TPU v7x, 32 devices: a whole 2x2x4 slice. The times are simulated.
32 devices in a mesh: dp: 4 (over z), expert: 8 (over y, x, core).
Axes of the slice: x: 2, y: 2, z: 4, core: 2. Of those that a mesh axis runs over, the one named last changes fastest.
Arguments:
- hidden: bfloat16 [3072, 2880], P('expert', 'dp'), may hold values from -6 to 6
- segments: int32 [8, 384], P('expert'), may hold values from 0 to 3, never falling along the last dimension, each value on 1 to 192 neighbouring positions
- request_adapter: int32 [8, 4], P('expert'), may hold values from 0 to 7
- routes: int32 [8, 384, 4], P('expert', 'dp'), may hold values from 0 to 7, all different within a row; in each aligned block of 96 rows (0 to 95, 96 to 191, ..., all dimensions but the last counted through in order) at most 64 rows name the same one
- expert_gates: bfloat16 [8, 384, 4], P('expert', 'dp'), may hold values from 0.049804688 to 0.59765625
- attention_gain: float32 [2880], replicated, may hold values from 0.25 to 1.75
- joined_weight: bfloat16 [2880, 4, 640], P(None, 'dp'), may hold values from -0.109375 to 0.109375
- sinks: float32 [32], P('dp'), may hold values from 0 to 3
- attention_out_weight: bfloat16 [2048, 2880], P('dp'), may hold values from -0.125 to 0.125
- joined_down_maps: bfloat16 [2880, 128], replicated, may hold values from -0.109375 to 0.109375
- joined_up_maps: bfloat16 [128, 4, 640], P(None, 'dp'), may hold values from -0.375 to 0.375
- output_down_maps: bfloat16 [2048, 128], P('dp'), may hold values from -0.125 to 0.125
- output_up_maps: bfloat16 [128, 2880], P(None, 'dp'), may hold values from -0.75 to 0.75
- expert_norm_gain: float32 [2880], replicated, may hold values from 0.25 to 1.75
- expert_gate_weight: bfloat16 [8, 2880, 2880], P('expert', None, 'dp'), may hold values from -0.109375 to 0.109375
- expert_up_weight: bfloat16 [8, 2880, 2880], P('expert', None, 'dp'), may hold values from -0.109375 to 0.109375
- expert_down_weight: bfloat16 [8, 2880, 2880], P('expert', 'dp'), may hold values from -0.109375 to 0.109375
- closing_gain: float32 [2880], replicated, may hold values from 0.25 to 1.75
- vocabulary_weight: bfloat16 [2880, 25600], P(None, ('dp', 'expert')), may hold values from -0.109375 to 0.109375
Outputs:
- hidden_out: bfloat16 [3072, 2880], P('expert', 'dp')
- logits: float32 [32, 25600], P(None, ('dp', 'expert'))
Inputs may be any that keep to these rules, and one draw needn't show every extreme that they name: `segments`: in each column the ids do not fall; each of the 4 requests has 1 to 192 tokens, and one has exactly 192. `routes`: the 4 experts of a token differ. Within the rows of one device (96 consecutive tokens, aligned blocks) no expert is named more than 64 times, and in some blocks one expert is named exactly 64 times.
All inputs are finite; a program needn't handle non-finite values.
Results may differ from a plain program's by a relative error of at most 0.02.
Values may be sent and summed in bfloat16 or wider, within the bound.
No kernel may reach another device: no remote copies, remote signals or barrier semaphores. Data moves between devices by JAX's collectives and lax.ppermute only.
A program may use at most 128 MiB of HBM per device.

v0:
```python
import jax
import jax.numpy as jnp
from jax import lax
from jax.sharding import PartitionSpec as P

HEAD_SIZE = 64
QUERY_GROUP = 8
TOP = 4
ADAPTER_RANK = 16
REQS = 4
epsilon = 1e-05
theta_base = 150000.0
adapter_scale = 2.0
glu_alpha = 1.702


def rms_scale(values, gain_row):
    mean_square = jnp.mean(values * values, axis=-1, keepdims=True)
    return values * lax.rsqrt(mean_square + epsilon) * gain_row


def positions_of(segment_row):
    counter = jnp.arange(segment_row.shape[0], dtype=jnp.int32)
    starting = jnp.concatenate(
        [jnp.ones((1,), dtype=jnp.bool_), segment_row[1:] != segment_row[:-1]]
    )
    first_index = lax.cummax(jnp.where(starting, counter, 0), axis=0)
    return counter - first_index


def adapter_per_token(segment_row, adapter_row):
    hits = segment_row[:, None] == jnp.arange(adapter_row.shape[0], dtype=jnp.int32)[None, :]
    return jnp.sum(jnp.where(hits, adapter_row[None, :], 0), axis=1)


def rotate_heads(values, positions):
    head_dim = values.shape[-1]
    half_dim = head_dim // 2
    frequency = theta_base ** (-2.0 * jnp.arange(half_dim, dtype=jnp.float32) / head_dim)
    angles = positions.astype(jnp.float32)[:, None] * frequency[None, :]
    cosine = jnp.cos(angles)[:, None, :]
    sine_part = jnp.sin(angles)[:, None, :]
    first_half = values[..., :half_dim]
    second_half = values[..., half_dim:]
    return jnp.concatenate(
        [
            first_half * cosine - second_half * sine_part,
            second_half * cosine + first_half * sine_part,
        ],
        axis=-1,
    )


def attend_heads(queries, key_heads, value_heads, segment_row, sink_row):
    tokens_now, kv_now, group_now, head_dim = queries.shape
    scores = jnp.einsum(
        "tkgh,skh->kgts", queries, key_heads, preferred_element_type=jnp.float32
    ) * head_dim ** (-0.5)
    counter = jnp.arange(tokens_now, dtype=jnp.int32)
    allowed = (segment_row[:, None] == segment_row[None, :]) & (
        counter[None, :] <= counter[:, None]
    )
    weights = jnp.where(allowed[None, None], jnp.exp(scores), 0.0)
    totals = jnp.sum(weights, axis=-1, keepdims=True) + jnp.exp(sink_row).reshape(
        kv_now, group_now, 1, 1
    )
    probs = (weights / totals).astype(jnp.bfloat16)
    blended_hidden = jnp.einsum(
        "kgts,skh->tkgh", probs, value_heads, preferred_element_type=jnp.float32
    )
    return blended_hidden.astype(jnp.bfloat16).reshape(tokens_now, kv_now * group_now * head_dim)


def shards(
    hidden,
    segments,
    request_adapter,
    routes,
    expert_gates,
    attention_gain,
    joined_weight,
    sinks,
    attention_out_weight,
    joined_down_maps,
    joined_up_maps,
    output_down_maps,
    output_up_maps,
    expert_norm_gain,
    expert_gate_weight,
    expert_up_weight,
    expert_down_weight,
    closing_gain,
    vocabulary_weight,
):
    groups = lax.axis_size("dp")
    columns = lax.axis_size("expert")
    position_dp = lax.axis_index("dp")
    segment_row = segments[0]
    adapter_row = request_adapter[0]
    col_tokens = segment_row.shape[0]
    gathered_rows = lax.all_gather(hidden, "dp", axis=1, tiled=True)
    width = gathered_rows.shape[1]
    normalized_hidden = rms_scale(gathered_rows.astype(jnp.float32), attention_gain).astype(
        jnp.bfloat16
    )
    joined_projection = jnp.dot(
        normalized_hidden, joined_weight.reshape(width, -1), preferred_element_type=jnp.float32
    )
    reduced_every_adapter = joined_down_maps.shape[1]
    reduced_hidden = jnp.dot(
        normalized_hidden, joined_down_maps, preferred_element_type=jnp.float32
    ).astype(jnp.bfloat16)
    rank_owner = jnp.arange(reduced_every_adapter, dtype=jnp.int32) // ADAPTER_RANK
    adapter_mask = adapter_per_token(segment_row, adapter_row)[:, None] == rank_owner[None, :]
    selected_reduced = jnp.where(adapter_mask, reduced_hidden, jnp.zeros_like(reduced_hidden))
    joined_projection = joined_projection + adapter_scale * jnp.dot(
        selected_reduced,
        joined_up_maps.reshape(reduced_every_adapter, -1),
        preferred_element_type=jnp.float32,
    )
    kv_here = joined_weight.shape[1]
    joined_projection = joined_projection.reshape(col_tokens, kv_here, QUERY_GROUP + 2, HEAD_SIZE)
    positions = positions_of(segment_row)
    queries = rotate_heads(
        joined_projection[:, :, :QUERY_GROUP].reshape(col_tokens, kv_here * QUERY_GROUP, HEAD_SIZE),
        positions,
    )
    queries = queries.astype(jnp.bfloat16).reshape(col_tokens, kv_here, QUERY_GROUP, HEAD_SIZE)
    key_heads = rotate_heads(joined_projection[:, :, QUERY_GROUP], positions).astype(jnp.bfloat16)
    value_heads = joined_projection[:, :, QUERY_GROUP + 1].astype(jnp.bfloat16)
    blended_hidden = attend_heads(queries, key_heads, value_heads, segment_row, sinks)
    partial_out = jnp.dot(blended_hidden, attention_out_weight, preferred_element_type=jnp.float32)
    mine_out = lax.psum_scatter(
        partial_out.astype(jnp.bfloat16), "dp", scatter_dimension=1, tiled=True
    ).astype(jnp.float32)
    output_reduced = lax.psum(
        jnp.dot(blended_hidden, output_down_maps, preferred_element_type=jnp.float32).astype(
            jnp.bfloat16
        ),
        "dp",
    )
    selected_output = jnp.where(adapter_mask, output_reduced, jnp.zeros_like(output_reduced))
    adapter_delta = adapter_scale * jnp.dot(
        selected_output, output_up_maps, preferred_element_type=jnp.float32
    )
    resid = (hidden.astype(jnp.float32) + mine_out + adapter_delta).astype(jnp.bfloat16)
    share = col_tokens // groups
    column_full = lax.all_gather(resid, "dp", axis=1, tiled=True)
    own_rows = lax.dynamic_slice_in_dim(column_full, position_dp * share, share, 0)
    moe_in = rms_scale(
        lax.optimization_barrier(own_rows).astype(jnp.float32), expert_norm_gain
    ).astype(jnp.bfloat16)
    experts = expert_gate_weight.shape[0] * columns
    capacity = 4 * share * TOP // (3 * experts)
    route_flat = routes[0].reshape(-1)
    one_hot = (route_flat[:, None] == jnp.arange(experts, dtype=jnp.int32)[None, :]).astype(
        jnp.int32
    )
    slot_rows = jnp.sum((jnp.cumsum(one_hot, axis=0) - one_hot) * one_hot, axis=1)
    target = route_flat * capacity + slot_rows
    source_rows = jnp.arange(route_flat.shape[0], dtype=jnp.int32) // TOP
    table = jnp.full((experts * capacity,), share, jnp.int32).at[target].set(source_rows)
    padded = jnp.concatenate([moe_in, jnp.zeros((1, width), jnp.bfloat16)], axis=0)
    outgoing = jnp.take(padded, table, axis=0).reshape(experts, capacity, width)
    gate_weight = expert_gate_weight[0]
    up_weight = expert_up_weight[0]
    down_weight = expert_down_weight[0]
    copies = jnp.tile(outgoing, (groups, 1, 1))
    arrived = lax.all_to_all(copies, ("dp", "expert"), split_axis=0, concat_axis=0, tiled=True)
    senders = arrived.shape[0]
    slots_now = arrived.shape[1]
    rows_in = arrived.reshape(-1, width)
    gate_part = jnp.dot(rows_in, gate_weight, preferred_element_type=jnp.float32)
    up_part = jnp.dot(rows_in, up_weight, preferred_element_type=jnp.float32)
    activated = (gate_part * jax.nn.sigmoid(glu_alpha * gate_part) * (up_part + 1.0)).astype(
        jnp.bfloat16
    )
    shares_out = (
        jnp.dot(activated, down_weight, preferred_element_type=jnp.float32)
        .astype(jnp.bfloat16)
        .reshape(senders, slots_now, width)
    )
    answers = lax.all_to_all(shares_out, ("dp", "expert"), split_axis=0, concat_axis=0, tiled=True)
    merged = jnp.sum(
        answers.reshape(groups, columns, capacity, width).astype(jnp.float32), axis=0
    ).astype(jnp.bfloat16)
    picked_out = jnp.take(merged.reshape(experts * capacity, width), target, axis=0).reshape(
        share, TOP, width
    )
    mixture = jnp.einsum(
        "tk,tkd->td", expert_gates[0], picked_out, preferred_element_type=jnp.float32
    )
    moe_rounded = lax.optimization_barrier(mixture.astype(jnp.bfloat16))
    finished = (own_rows.astype(jnp.float32) + moe_rounded.astype(jnp.float32)).astype(jnp.bfloat16)
    hidden_out = lax.all_to_all(finished, "dp", split_axis=1, concat_axis=0, tiled=True)
    counter = jnp.arange(col_tokens, dtype=jnp.int32)
    request_ids = jnp.arange(REQS, dtype=jnp.int32)
    last_index = jnp.max(
        jnp.where(segment_row[None, :] == request_ids[:, None], counter[None, :], -1), axis=1
    )
    local_index = last_index - position_dp * share
    inside = (local_index >= 0) & (local_index < share)
    chosen = jnp.take(finished, jnp.clip(local_index, 0, share - 1), axis=0)
    chosen = jnp.where(inside[:, None], chosen, jnp.zeros_like(chosen))
    ends = rms_scale(chosen.astype(jnp.float32), closing_gain).astype(jnp.bfloat16)
    spread_rows = lax.all_gather(ends, ("dp", "expert"), axis=0, tiled=True)
    tail_rows = jnp.sum(
        spread_rows.reshape(groups, columns * REQS, width).astype(jnp.float32), axis=0
    ).astype(jnp.bfloat16)
    logits = jnp.dot(tail_rows, vocabulary_weight, preferred_element_type=jnp.float32)
    return (hidden_out, logits)


def solution(mesh):
    in_specs = (
        P("expert", "dp"),
        P("expert", None),
        P("expert", None),
        P("expert", "dp", None),
        P("expert", "dp", None),
        P(),
        P(None, "dp", None),
        P("dp"),
        P("dp", None),
        P(),
        P(None, "dp", None),
        P("dp", None),
        P(None, "dp"),
        P(),
        P("expert", None, "dp"),
        P("expert", None, "dp"),
        P("expert", "dp", None),
        P(),
        P(None, ("dp", "expert")),
    )
    out_specs = (P("expert", "dp"), P(None, ("dp", "expert")))
    return jax.shard_map(shards, mesh=mesh, in_specs=in_specs, out_specs=out_specs, check_vma=False)
```

profile of v0, /device:TPU:0, one launch (start us, length us, event | category | flops | bytes accessed | tf_op | source)
XLA Modules:
  0.0 916.7 jit_solution(5084641404369946867)
XLA Ops:
  12.1 48.3 %all-gather.4.cloned.1.call-done = bf16[384,2880]{0,1:T(8,128)(2,1)} async-done(((bf16[384,720]{0,1:T(8,128)(2,1)}), bf16[384,2880]{0,1:T(8,128)(2,1)}) %all-gather.4.cloned.1.call-update) | async-done | bytes 2211856 | tf_op jit(solution)/shard_map/all_gather | solution.py:101
  60.4 2.2 fusion
  62.6 5.9 fusion.11
  68.5 4.8 fusion.21
  73.3 2.5 copy.59
  79.6 2.2 fusion.23
  83.7 4.1 convolution_convert_fusion.1
  87.9 29.0 %all-reduce.3.cloned.1.call-done = bf16[384,128]{1,0:T(8,128)(2,1)} async-done(((bf16[384,128]{1,0:T(8,128)(2,1)}), bf16[384,128]{1,0:T(8,128)(2,1)}) %all-reduce.3.cloned.1.call-update) | async-done | bytes 98320 | tf_op jit(solution)/shard_map/psum | solution.py:136
  116.8 48.0 %reduce-scatter.2.cloned.1.call-done = bf16[384,720]{0,1:T(8,128)(2,1)} async-done(((bf16[384,2880]{0,1:T(8,128)(2,1)}), bf16[384,720]{0,1:T(8,128)(2,1)}) %reduce-scatter.2.cloned.1.call-update) | async-done | bytes 552976 | tf_op jit(solution)/shard_map/reduce_scatter | solution.py:133
  164.9 2.4 fusion.22
  169.2 3.1 scatter_custom_fusion
  172.4 42.6 %all-gather.6.cloned.1.call-done = bf16[384,2880]{0,1:T(8,128)(2,1)} async-done(((bf16[384,720]{0,1:T(8,128)(2,1)}), bf16[384,2880]{0,1:T(8,128)(2,1)}) %all-gather.6.cloned.1.call-update) | async-done | bytes 2211856 | tf_op jit(solution)/shard_map/all_gather | solution.py:148
  215.0 1.7 constant_dynamic-slice_fusion
  217.9 3.7 gather_fusion
  221.6 2.2 broadcast_select_fusion
  223.8 6.0 tile.8
  229.8 266.5 %all_to_all.29 = bf16[32,64,2880]{2,1,0:T(8,128)(2,1)} all-to-all(bf16[32,64,2880]{2,1,0:T(8,128)(2,1)} %bitcast.115), channel_id=1, replica_groups=mesh['dp'=4,'expert'=8] {'dp','expert'}, dimensions={0} | all-to-all | bytes 23592960 | tf_op jit(solution)/shard_map/all_to_all | solution.py:169
  496.3 15.1 %fusion.4 = f32[2048,720]{0,1:T(8,128)} fusion(bf16[2048,2880]{1,0:T(8,128)(2,1)} %bitcast.26, bf16[1,2880,720]{1,2,0:T(8,128)(2,1)} %param.34), kind=kOutput, calls=%fused_computation.15 | convolution fusion | flops 8493465600 | bytes 21841920 | tf_op jit(solution)/shard_map/dot_general | solution.py:174
  511.4 26.6 %convolution_convert_fusion = bf16[2048,2880]{0,1:T(8,128)(2,1)} fusion(bf16[1,720,2880]{2,1,0:T(8,128)(2,1)} %param.35, f32[2048,720]{0,1:T(8,128)} %fusion.4, bf16[2048,2880]{1,0:T(8,128)(2,1)} %bitcast.26, bf16[1,2880,720]{1,2,0:T(8,128)(2,1)} %param.33), kind=kOutput, calls=%fused_computation.4 | convolution fusion | flops 17004625920 | bytes 37785600 | tf_op jit(solution)/shard_map/dot_general | solution.py:179
  538.0 16.3 %copy.67 = bf16[2048,2880]{1,0:T(8,128)(2,1)} copy(bf16[2048,2880]{0,1:T(8,128)(2,1)} %convolution_convert_fusion) | data formatting | bytes 23592960 | tf_op jit(solution)/shard_map/convert_element_type | solution.py:180
  554.4 4.1 all-to-all-start.1
  559.1 266.6 %all-to-all-done.1 = bf16[32,64,2880]{2,1,0:T(8,128)(2,1)} async-done(((bf16[32,64,2880]{2,1,0:T(8,128)(2,1)}), bf16[32,64,2880]{2,1,0:T(8,128)(2,1)}, u32[]{:S(2)}, u32[]{:S(2)}) %all-to-all-start.1) | async-done | bytes 11796512 | tf_op jit(solution)/shard_map/all_to_all | solution.py:183
  825.7 6.8 reduce_sum.89
  832.5 3.5 gather_fusion.1
  836.0 2.6 gather.19
  838.6 4.7 multiply_reduce_fusion
  843.6 1.7 add_convert_fusion
  847.6 3.5 all-to-all-start.2
  851.2 49.2 %all-gather = bf16[32,4,2880]{2,1,0:T(4,128)(2,1)} all-gather(bf16[1,4,2880]{2,1,0:T(4,128)(2,1)S(1)} %fusion.60), channel_id=1, replica_groups=mesh['dp'=4,'expert'=8] {'dp','expert'}, dimensions={0}, use_global_device_ids=true | all-gather | bytes 760320 | tf_op jit(solution)/shard_map/all_gather | solution.py:206
  900.4 2.3 reshape.444
  902.7 2.0 reduce_sum.91
  904.6 4.5 fusion.79
  (94 shorter events, 18.0 us)
Async XLA Ops:
  7.2 76.5 %copy-start = (bf16[512,2880]{0,1:T(8,128)(2,1)S(1)}, bf16[512,2880]{0,1:T(8,128)(2,1)}, u32[]{:S(2)}) copy-start(bf16[512,2880]{0,1:T(8,128)(2,1)} %param.27) | copy-start | bytes 8847364
  7.2 53.2 %all-gather.4.cloned.1.call-start = ((), (), s32[]{:S(2)}) async-start(), calls=%async_computation.4 | async-start | bytes 2764800 | tf_op jit(solution)/shard_map/all_gather | solution.py:101
  7.9 108.9 %all-reduce.3.cloned.1.call-start = ((), (), s32[]{:S(2)}) async-start(), calls=%async_computation.6 | async-start | bytes 196608 | tf_op jit(solution)/shard_map/psum | solution.py:136
  62.6 6.0 copy-start.9
  62.6 6.0 copy-start.10
  79.6 3.0 copy-start.4
  81.9 0.8 copy-start.3
  83.6 81.3 %copy-start.2 = (bf16[384,720]{0,1:T(8,128)(2,1)S(1)}, bf16[384,720]{0,1:T(8,128)(2,1)}, u32[]{:S(2)}) copy-start(bf16[384,720]{0,1:T(8,128)(2,1)} %param.19) | copy-start | bytes 1658884
  83.6 81.3 %reduce-scatter.2.cloned.1.call-start = ((), (), s32[]{:S(2)}) async-start(), calls=%async_computation.5 | async-start | bytes 2764800 | tf_op jit(solution)/shard_map/reduce_scatter | solution.py:133
  87.8 79.6 %copy-start.5 = (s32[1,96,4]{1,2,0:T(4,128)S(1)}, s32[1,96,4]{1,2,0:T(4,128)}, u32[]{:S(2)}) copy-start(s32[1,96,4]{1,2,0:T(4,128)} %param.22) | copy-start | bytes 4612
  87.8 129.3 %copy-start.6 = (f32[2880]{0:T(1024)S(1)}, f32[2880]{0:T(1024)}, u32[]{:S(2)}) copy-start(f32[2880]{0:T(1024)} %param.32) | copy-start | bytes 34564
  87.8 127.2 %all-gather.6.cloned.1.call-start = ((), (), s32[]{:S(2)}) async-start(), calls=%async_computation.7 | async-start | bytes 2764800 | tf_op jit(solution)/shard_map/all_gather | solution.py:148
  554.4 4.4 copy-start.8
  554.4 271.3 %all-to-all-start.1 = ((bf16[32,64,2880]{2,1,0:T(8,128)(2,1)}), bf16[32,64,2880]{2,1,0:T(8,128)(2,1)}, u32[]{:S(2)}, u32[]{:S(2)}) async-start(bf16[32,64,2880]{2,1,0:T(8,128)(2,1)} %bitcast.114), calls=%async_computation.2 | async-start | bytes 24117248 | tf_op jit(solution)/shard_map/all_to_all | solution.py:183
  843.2 7.8 copy-start.7
  847.6 61.5 %all-to-all-start.2 = ((bf16[96,4,720]{2,0,1:T(8,128)(2,1)}), bf16[96,4,720]{2,0,1:T(8,128)(2,1)S(1)}, u32[]{:S(2)}, u32[]{:S(2)}) async-start(bf16[96,4,720]{2,0,1:T(8,128)(2,1)} %copy.68), calls=%async_computation.3 | async-start | bytes 1179648 | tf_op jit(solution)/shard_map/all_to_all | solution.py:195
  851.2 59.0 %copy-start.1 = (bf16[512,2880]{0,1:T(8,128)(2,1)S(1)}, bf16[512,2880]{0,1:T(8,128)(2,1)}, u32[]{:S(2)}) copy-start(bf16[512,2880]{0,1:T(8,128)(2,1)} %param.27) | copy-start | bytes 8847364
Sparse Core Ops, SparseCore 0:
  9.6 50.7 all-gather.3
  83.7 33.0 all-reduce.2
  119.3 45.5 reduce-scatter.1
  167.5 47.4 all-gather.5
where the time goes:
time: 918 us; the launch traced here: 917 us
  waiting for transfers between devices  435 us (47%)
  blocking collectives  316 us (34%)
  matrix products  68 us (7%)
  local copies, waits for them, and re-layouts  50.3 us (5%)
  other arithmetic  25.7 us (3%)
  between operations  14.1 us (2%)
    all_to_all x1, waiting for transfers between devices, shards(): lax.all_to_all(shares_out, ('dp', 'expert'), split_axis=0, concat_axis=0,...  267 us
    all_to_all x1, blocking collectives, shards(): lax.all_to_all(copies, ('dp', 'expert'), split_axis=0, concat_axis=0, til...  266 us
    all_gather x1, blocking collectives, shards(): spread_rows = lax.all_gather(ends, ('dp', 'expert'), axis=0, tiled=True)  49.2 us
    all_gather x1, waiting for transfers between devices, shards(): gathered_rows = lax.all_gather(hidden, 'dp', axis=1, tiled=True)  48.3 us
    reduce_scatter x1, waiting for transfers between devices, shards(): lax.psum_scatter(partial_out.astype(jnp.bfloat16), 'dp', scatter_dimensio...  48 us
    all_gather x1, waiting for transfers between devices, shards(): column_full = lax.all_gather(resid, 'dp', axis=1, tiled=True)  42.6 us
    psum x1, waiting for transfers between devices, shards(): lax.psum(jnp.dot(blended_hidden, output_down_maps, preferred_element_type...  29 us
    dot_general x1, matrix products, shards(): jnp.dot(activated, down_weight, preferred_element_type=jnp.float32)  26.6 us
  transfers between devices with their start and end apart: 6, of which 5 were waited for; matrix products, arithmetic and copies ran while one was open for 2% of the time, Pallas kernels for 0%

commit v1 on v0

--- a/solution.py
+++ b/solution.py
@@ -145,7 +145,14 @@
     )
     resid = (hidden.astype(jnp.float32) + mine_out + adapter_delta).astype(jnp.bfloat16)
     share = col_tokens // groups
-    column_full = lax.all_gather(resid, "dp", axis=1, tiled=True)
+    ways, here, step = (lax.axis_size("dp"), lax.axis_index("dp"), resid.shape[1])
+    line, have = (resid, 1)
+    while have < ways:
+        line = jnp.concatenate(
+            [line, lax.ppermute(line, "dp", [(d, (d - have) % ways) for d in range(ways)])], axis=1
+        )
+        have = 2 * have
+    column_full = jnp.roll(line, here * step, axis=1)
     own_rows = lax.dynamic_slice_in_dim(column_full, position_dp * share, share, 0)
     moe_in = rms_scale(
         lax.optimization_barrier(own_rows).astype(jnp.float32), expert_norm_gain

time: 918 us -> 956 us (1.041)
  starting transfers between devices: 7.73 us -> 20.7 us
  waiting for transfers between devices: 435 us -> 447 us
    ppermute x0 -> x2, waiting for transfers between devices: none -> 54.6 us  [shards(): lax.ppermute(line, 'dp', [(d, (d - have) % ways) for d in range(ways)])]
    all_gather x1 -> x0, waiting for transfers between devices: 42.6 us -> none  [shards(): column_full = lax.all_gather(resid, 'dp', axis=1, tiled=True)]
    ppermute x0 -> x2, starting transfers between devices: none -> 13 us  [shards(): lax.ppermute(line, 'dp', [(d, (d - have) % ways) for d in range(ways)])]
  transfers between devices with their start and end apart: 6 -> 7, of which waited for: 5 -> 6; matrix products, arithmetic and copies ran while one was open for 2% -> 2% of each run, Pallas kernels for 0% -> 0%
where the time goes in v1:
time: 956 us; the launch traced here: 947 us
  waiting for transfers between devices  447 us (47%)
  blocking collectives  317 us (33%)
  matrix products  66.8 us (7%)
  local copies, waits for them, and re-layouts  55.2 us (6%)
  other arithmetic  26 us (3%)
  starting transfers between devices  20.7 us (2%)
  between operations  14.5 us (2%)
    all_to_all x1, blocking collectives, shards(): lax.all_to_all(copies, ('dp', 'expert'), split_axis=0, concat_axis=0, til...  268 us
    all_to_all x1, waiting for transfers between devices, shards(): lax.all_to_all(shares_out, ('dp', 'expert'), split_axis=0, concat_axis=0,...  267 us
    ppermute x2, waiting for transfers between devices, shards(): lax.ppermute(line, 'dp', [(d, (d - have) % ways) for d in range(ways)])  54.6 us
    all_gather x1, blocking collectives, shards(): spread_rows = lax.all_gather(ends, ('dp', 'expert'), axis=0, tiled=True)  49.2 us
    all_gather x1, waiting for transfers between devices, shards(): gathered_rows = lax.all_gather(hidden, 'dp', axis=1, tiled=True)  48.3 us
    reduce_scatter x1, waiting for transfers between devices, shards(): lax.psum_scatter(partial_out.astype(jnp.bfloat16), 'dp', scatter_dimensio...  48 us
    psum x1, waiting for transfers between devices, shards(): lax.psum(jnp.dot(blended_hidden, output_down_maps, preferred_element_type...  29 us
    dot_general x1, matrix products, shards(): jnp.dot(activated, down_weight, preferred_element_type=jnp.float32)  26.6 us
  transfers between devices with their start and end apart: 7, of which 6 were waited for; matrix products, arithmetic and copies ran while one was open for 2% of the time, Pallas kernels for 0%

profile of v1, /device:TPU:0, one launch (start us, length us, event | category | flops | bytes accessed | tf_op | source)
XLA Modules:
  0.0 947.4 jit_solution(6750126829561829352)
XLA Ops:
  12.1 48.3 %all-gather.3.cloned.1.call-done = bf16[384,2880]{0,1:T(8,128)(2,1)} async-done(((bf16[384,720]{0,1:T(8,128)(2,1)}), bf16[384,2880]{0,1:T(8,128)(2,1)}) %all-gather.3.cloned.1.call-update) | async-done | bytes 2211856 | tf_op jit(solution)/shard_map/all_gather | solution.py:101
  60.4 2.2 fusion
  62.6 5.9 fusion.11
  68.5 4.8 fusion.21
  73.3 2.5 copy.59
  79.6 2.2 fusion.23
  83.7 4.1 convolution_convert_fusion.1
  87.8 29.0 %all-reduce.3.cloned.1.call-done = bf16[384,128]{1,0:T(8,128)(2,1)} async-done(((bf16[384,128]{1,0:T(8,128)(2,1)}), bf16[384,128]{1,0:T(8,128)(2,1)}) %all-reduce.3.cloned.1.call-update) | async-done | bytes 98320 | tf_op jit(solution)/shard_map/psum | solution.py:136
  116.9 48.0 %reduce-scatter.2.cloned.1.call-done = bf16[384,720]{0,1:T(8,128)(2,1)} async-done(((bf16[384,2880]{0,1:T(8,128)(2,1)}), bf16[384,720]{0,1:T(8,128)(2,1)}) %reduce-scatter.2.cloned.1.call-update) | async-done | bytes 552976 | tf_op jit(solution)/shard_map/reduce_scatter | solution.py:133
  164.9 2.5 constant_dynamic-update-slice_fusion.5
  167.4 10.9 %collective-permute-start = (bf16[384,720]{0,1:T(8,128)(2,1)S(1)}, bf16[384,720]{0,1:T(8,128)(2,1)S(1)}, u32[]{:S(2)}, u32[]{:S(2)}) collective-permute-start(bf16[384,720]{0,1:T(8,128)(2,1)S(1)} %get-tuple-element.23), channel_id=1, source_target_pairs={{0,24},{8,0},{16,8},{24,16},{1,25},{9,1},{17,9},{25,17},{2,26},{10... | collective-permute-start | bytes 1658888 | tf_op jit(solution)/shard_map/ppermute | solution.py:152
  179.6 11.4 %collective-permute-done = bf16[384,720]{0,1:T(8,128)(2,1)S(1)} collective-permute-done((bf16[384,720]{0,1:T(8,128)(2,1)S(1)}, bf16[384,720]{0,1:T(8,128)(2,1)S(1)}, u32[]{:S(2)}, u32[]{:S(2)}) %collective-permute-start) | collective-permute-done | bytes 552992 | tf_op jit(solution)/shard_map/ppermute | solution.py:152
  191.1 2.1 collective-permute-start.1
  193.8 2.9 scatter_custom_fusion
  197.7 43.2 %collective-permute-done.1 = bf16[384,1440]{0,1:T(8,128)(2,1)S(1)} collective-permute-done((bf16[384,1440]{0,1:T(8,128)(2,1)S(1)}, bf16[384,1440]{0,1:T(8,128)(2,1)S(1)}, u32[]{:S(2)}, u32[]{:S(2)}) %collective-permute-start.1) | collective-permute-done | bytes 1105952 | tf_op jit(solution)/shard_map/ppermute | solution.py:152
  247.9 3.7 gather_fusion
  251.6 2.2 broadcast_select_fusion
  253.9 6.0 tile.8
  259.9 267.9 %all_to_all.29 = bf16[32,64,2880]{2,1,0:T(8,128)(2,1)} all-to-all(bf16[32,64,2880]{2,1,0:T(8,128)(2,1)} %bitcast.115), channel_id=1, replica_groups=mesh['dp'=4,'expert'=8] {'dp','expert'}, dimensions={0} | all-to-all | bytes 23592960 | tf_op jit(solution)/shard_map/all_to_all | solution.py:176
  527.8 13.9 %fusion.4 = f32[2048,720]{0,1:T(8,128)} fusion(bf16[2048,2880]{1,0:T(8,128)(2,1)} %bitcast.26, bf16[1,2880,720]{1,2,0:T(8,128)(2,1)S(1)} %bitcast.127), kind=kOutput, calls=%fused_computation.15 | convolution fusion | flops 8493465600 | bytes 21841920 | tf_op jit(solution)/shard_map/dot_general | solution.py:181
  541.6 26.6 %convolution_convert_fusion = bf16[2048,2880]{0,1:T(8,128)(2,1)} fusion(bf16[1,720,2880]{2,1,0:T(8,128)(2,1)} %param.35, f32[2048,720]{0,1:T(8,128)} %fusion.4, bf16[2048,2880]{1,0:T(8,128)(2,1)} %bitcast.26, bf16[1,2880,720]{1,2,0:T(8,128)(2,1)} %param.33), kind=kOutput, calls=%fused_computation.4 | convolution fusion | flops 17004625920 | bytes 37785600 | tf_op jit(solution)/shard_map/dot_general | solution.py:186
  568.3 16.3 %copy.67 = bf16[2048,2880]{1,0:T(8,128)(2,1)} copy(bf16[2048,2880]{0,1:T(8,128)(2,1)} %convolution_convert_fusion) | data formatting | bytes 23592960 | tf_op jit(solution)/shard_map/convert_element_type | solution.py:187
  584.6 4.1 all-to-all-start.1
  589.3 266.6 %all-to-all-done.1 = bf16[32,64,2880]{2,1,0:T(8,128)(2,1)} async-done(((bf16[32,64,2880]{2,1,0:T(8,128)(2,1)}), bf16[32,64,2880]{2,1,0:T(8,128)(2,1)}, u32[]{:S(2)}, u32[]{:S(2)}) %all-to-all-start.1) | async-done | bytes 11796512 | tf_op jit(solution)/shard_map/all_to_all | solution.py:190
  855.9 6.8 reduce_sum.89
  862.7 3.5 gather_fusion.1
  866.2 2.6 gather.19
  868.8 4.7 multiply_reduce_fusion
  878.0 3.5 all-to-all-start.2
  881.5 49.2 %all-gather = bf16[32,4,2880]{2,1,0:T(4,128)(2,1)} all-gather(bf16[1,4,2880]{2,1,0:T(4,128)(2,1)S(1)} %fusion.60), channel_id=1, replica_groups=mesh['dp'=4,'expert'=8] {'dp','expert'}, dimensions={0}, use_global_device_ids=true | all-gather | bytes 760320 | tf_op jit(solution)/shard_map/all_gather | solution.py:213
  930.7 2.3 reshape.444
  935.0 4.5 fusion.79
  (105 shorter events, 28.6 us)
Async XLA Ops:
  7.2 76.5 %copy-start = (bf16[512,2880]{0,1:T(8,128)(2,1)S(1)}, bf16[512,2880]{0,1:T(8,128)(2,1)}, u32[]{:S(2)}) copy-start(bf16[512,2880]{0,1:T(8,128)(2,1)} %param.27) | copy-start | bytes 8847364
  7.2 53.2 %all-gather.3.cloned.1.call-start = ((), (), s32[]{:S(2)}) async-start(), calls=%async_computation.4 | async-start | bytes 2764800 | tf_op jit(solution)/shard_map/all_gather | solution.py:101
  7.9 109.0 %all-reduce.3.cloned.1.call-start = ((), (), s32[]{:S(2)}) async-start(), calls=%async_computation.6 | async-start | bytes 196608 | tf_op jit(solution)/shard_map/psum | solution.py:136
  62.6 6.0 copy-start.9
  62.6 6.0 copy-start.10
  79.6 3.0 copy-start.4
  81.9 0.8 copy-start.3
  83.6 81.3 %copy-start.2 = (bf16[384,720]{0,1:T(8,128)(2,1)S(1)}, bf16[384,720]{0,1:T(8,128)(2,1)}, u32[]{:S(2)}) copy-start(bf16[384,720]{0,1:T(8,128)(2,1)} %param.19) | copy-start | bytes 1658884
  83.6 81.3 %reduce-scatter.2.cloned.1.call-start = ((), (), s32[]{:S(2)}) async-start(), calls=%async_computation.5 | async-start | bytes 2764800 | tf_op jit(solution)/shard_map/reduce_scatter | solution.py:133
  87.8 90.5 %copy-start.5 = (s32[1,96,4]{1,2,0:T(4,128)S(1)}, s32[1,96,4]{1,2,0:T(4,128)}, u32[]{:S(2)}) copy-start(s32[1,96,4]{1,2,0:T(4,128)} %param.22) | copy-start | bytes 4612
  167.4 23.6 %collective-permute-start = (bf16[384,720]{0,1:T(8,128)(2,1)S(1)}, bf16[384,720]{0,1:T(8,128)(2,1)S(1)}, u32[]{:S(2)}, u32[]{:S(2)}) collective-permute-start(bf16[384,720]{0,1:T(8,128)(2,1)S(1)} %get-tuple-element.23), channel_id=1, source_target_pairs={{0,24},{8,0},{16,8},{24,16},{1,25},{9,1},{17,9},{25,17},{2,26},{10... | collective-permute-start | bytes 1658888 | tf_op jit(solution)/shard_map/ppermute | solution.py:152
  191.1 49.7 %collective-permute-start.1 = (bf16[384,1440]{0,1:T(8,128)(2,1)S(1)}, bf16[384,1440]{0,1:T(8,128)(2,1)S(1)}, u32[]{:S(2)}, u32[]{:S(2)}) collective-permute-start(bf16[384,1440]{0,1:T(8,128)(2,1)S(1)} %pad_maximum_fusion), channel_id=1, source_target_pairs={{0,16},{8,24},{16,0},{24,8},{1,17},{9,25},{17,1},{25,9},{2,18},{10... | collective-permute-start | bytes 3317768 | tf_op jit(solution)/shard_map/ppermute | solution.py:152
  197.7 49.4 %copy-start.6 = (f32[2880]{0:T(1024)S(1)}, f32[2880]{0:T(1024)}, u32[]{:S(2)}) copy-start(f32[2880]{0:T(1024)} %param.32) | copy-start | bytes 34564
  253.9 273.9 %slice-start = ((s8[4239360]{0:T(1024)(128)(4,1)}), s8[45056]{0:T(1024)(128)(4,1)S(1)}, s32[]{:S(2)}) async-start(s8[4239360]{0:T(1024)(128)(4,1)} %bitcast.126), calls=%async_computation.7 | async-start | bytes 90112
  259.9 267.9 %slice-start.1 = ((s8[4239360]{0:T(1024)(128)(4,1)}), s8[4194304]{0:T(1024)(128)(4,1)S(1)}, s32[]{:S(2)}) async-start(s8[4239360]{0:T(1024)(128)(4,1)} %bitcast.126), calls=%async_computation.8 | async-start | bytes 8388608
  584.6 4.4 copy-start.8
  584.6 271.3 %all-to-all-start.1 = ((bf16[32,64,2880]{2,1,0:T(8,128)(2,1)}), bf16[32,64,2880]{2,1,0:T(8,128)(2,1)}, u32[]{:S(2)}, u32[]{:S(2)}) async-start(bf16[32,64,2880]{2,1,0:T(8,128)(2,1)} %bitcast.114), calls=%async_computation.2 | async-start | bytes 24117248 | tf_op jit(solution)/shard_map/all_to_all | solution.py:190
  873.4 8.0 copy-start.7
  878.0 61.5 %all-to-all-start.2 = ((bf16[96,4,720]{2,0,1:T(8,128)(2,1)}), bf16[96,4,720]{2,0,1:T(8,128)(2,1)S(1)}, u32[]{:S(2)}, u32[]{:S(2)}) async-start(bf16[96,4,720]{2,0,1:T(8,128)(2,1)} %copy.68), calls=%async_computation.3 | async-start | bytes 1179648 | tf_op jit(solution)/shard_map/all_to_all | solution.py:202
  881.5 59.0 %copy-start.1 = (bf16[512,2880]{0,1:T(8,128)(2,1)S(1)}, bf16[512,2880]{0,1:T(8,128)(2,1)}, u32[]{:S(2)}) copy-start(bf16[512,2880]{0,1:T(8,128)(2,1)} %param.27) | copy-start | bytes 8847364
Sparse Core Ops, SparseCore 0:
  9.6 50.7 all-gather.2
  83.7 33.1 all-reduce.2
  119.3 45.5 reduce-scatter.1
